TPU v7x, 256 devices: a whole 4x4x8 slice. The times are simulated.
256 devices in a mesh: ctx: 32 (over y, x, core), head: 8 (over z).
Axes of the slice: x: 4, y: 4, z: 8, core: 2. Of those that a mesh axis runs over, the one named last changes fastest.
Arguments:
- ssm_input: bfloat16 [8192, 8192], P('ctx', 'head'), may hold values from -6 to 6
- gate_input: bfloat16 [8192, 8192], P('ctx', 'head'), may hold values from -6 to 6
- step_raw: float32 [8192, 128], P('ctx', 'head'), may hold values from -4 to 4
- b_matrix: bfloat16 [8192, 1024], P('ctx', 'head'), may hold values from -6 to 6
- c_matrix: bfloat16 [8192, 1024], P('ctx', 'head'), may hold values from -6 to 6
- step_bias: float32 [128], P('head'), may hold values from -6 to -4
- log_rate: float32 [128], P('head')
- skip_gain: float32 [128], P('head'), may hold values from 0.5 to 1.5
- norm_weight: float32 [8192], P('head'), may hold values from 0.5 to 1.5
- doc_resets: int32 [8192], P('ctx'), may hold values from 0 to 1, as said below
- grad_output: bfloat16 [8192, 8192], P('ctx', 'head'), may hold values from -6 to 6
Outputs:
- grad_input: bfloat16 [8192, 8192], P('ctx', 'head')
- grad_gate: bfloat16 [8192, 8192], P('ctx', 'head')
- grad_step: float32 [8192, 128], P('ctx', 'head')
- grad_b_matrix: float32 [8192, 1024], P('ctx', 'head')
- grad_c_matrix: float32 [8192, 1024], P('ctx', 'head')
Inputs may be any that keep to these rules, and one draw needn't show every extreme that they name: `doc_resets`: exactly 4 positions hold 1, all of them among positions 1 to 127; all others hold 0.
All inputs are finite; a program needn't handle non-finite values.
Results may differ from a plain program's by a relative error of at most 0.001.
Values sent between devices are 32-bit elements; how exact they have to be, the bound alone decides.
No kernel may reach another device: no remote copies, remote signals or barrier semaphores. Data moves between devices by JAX's collectives and lax.ppermute only.
A program may use at most 64 MiB of HBM per device.

v0:
```python
import jax
import jax.numpy as jnp
from jax import lax
from jax.sharding import PartitionSpec as P

HEAD_DIM = 64
STATE = 128
SPAN = 256
HIGHEST_PRECISION = lax.Precision.HIGHEST
EPSILON = 1e-05


def carried_in(array, axis, combine, identity):
    size, index = (lax.axis_size(axis), lax.axis_index(axis))
    everything = jax.tree.map(lambda part: lax.all_gather(part, axis), array)
    start = jax.tree.map(
        lambda part, zero: jnp.broadcast_to(jnp.asarray(zero, part.dtype), part.shape),
        array,
        identity,
    )

    def turn(k, before):
        at = size - 1 - k
        reached = at > index
        new = combine(before, jax.tree.map(lambda part: part[at], everything))
        return jax.tree.map(lambda a, b: jnp.where(reached, a, b), new, before)

    return lax.fori_loop(0, size, turn, start)


def span_mix(x_span, dt_span, b_span, c_span, log_cum, segment):
    log_rows = jnp.moveaxis(log_cum, 0, -1)
    spread = log_rows[..., :, None] - log_rows[..., None, :]
    places = jnp.arange(x_span.shape[0], dtype=jnp.int32)
    keep_mask = (
        (places[:, None] >= places[None, :]) & (segment[:, None] == segment[None, :])
    ).astype(jnp.float32)
    masked = jnp.exp(jnp.minimum(spread, 0.0)) * keep_mask
    scores = jnp.einsum("tgn,sgn->gts", c_span, b_span, precision=HIGHEST_PRECISION)
    weights = scores[:, None] * masked * jnp.moveaxis(dt_span, 0, -1)[..., None, :]
    return jnp.einsum("ghts,sghp->tghp", weights, x_span, precision=HIGHEST_PRECISION)


def block_decays(dt_spans, segment, decay_rate):
    log_cum = jnp.cumsum(dt_spans * decay_rate, axis=1)
    closing = segment[:, -1]
    through = jnp.exp(log_cum[:, -1]) * (closing == 0).astype(jnp.float32)[:, None, None]
    return (log_cum, closing, through)


def local_states(x_spans, dt_spans, b_spans, segment, decay_rate):
    log_cum, closing, through = block_decays(dt_spans, segment, decay_rate)
    same_doc = (segment == closing[:, None]).astype(jnp.float32)
    tail_decay = jnp.exp(log_cum[:, -1:] - log_cum) * same_doc[:, :, None, None]
    added_terms = jnp.einsum(
        "kqgh,kqghp,kqgn->kghpn",
        tail_decay * dt_spans,
        x_spans,
        b_spans,
        precision=HIGHEST_PRECISION,
    )

    def advance(carried_pair, item_pair):
        carry_state, product = carried_pair
        decay_now, fresh_state = item_pair
        return (
            (decay_now[..., None, None] * carry_state + fresh_state, product * decay_now),
            carry_state,
        )

    initial = (
        jnp.zeros(added_terms.shape[1:], jnp.float32),
        jnp.ones(through.shape[1:], jnp.float32),
    )
    (final_state, product), starts = lax.scan(advance, initial, (through, added_terms))
    return (starts, final_state, product)


def output_part(x_spans, dt_spans, b_spans, c_spans, segment, decay_rate, starts, entry_state):
    log_cum, closing, through = block_decays(dt_spans, segment, decay_rate)

    def rolling(product, decay_now):
        return (product * decay_now, product)

    _, before = lax.scan(rolling, jnp.ones(through.shape[1:], jnp.float32), through)
    full_start = starts + before[..., None, None] * entry_state[None]
    opened = (segment == 0).astype(jnp.float32)
    entry_decay = jnp.exp(log_cum) * opened[:, :, None, None]
    carried = (
        jnp.einsum("kqgn,kghpn->kqghp", c_spans, full_start, precision=HIGHEST_PRECISION)
        * entry_decay[..., None]
    )
    mix_block = jax.checkpoint(lambda pieces: span_mix(*pieces))
    inner_part = lax.map(mix_block, (x_spans, dt_spans, b_spans, c_spans, log_cum, segment))
    return inner_part + carried


def compose(earlier, later):
    decay_early, sum_early = earlier
    decay_late, sum_late = later
    return (decay_early * decay_late, decay_late[..., None, None] * sum_early + sum_late)


def body(
    ssm_input,
    gate_input,
    step_raw,
    b_matrix,
    c_matrix,
    step_bias,
    log_rate,
    skip_gain,
    norm_weight,
    doc_resets,
    grad_output,
):
    tokens_here = ssm_input.shape[0]
    heads_here = step_raw.shape[1]
    groups_here = b_matrix.shape[1] // STATE
    per_group = heads_here // groups_here
    spans = tokens_here // SPAN
    x_float = ssm_input.astype(jnp.float32)
    gate_float = gate_input.astype(jnp.float32)
    shifted = step_raw + step_bias[None, :]
    step_size = jax.nn.softplus(shifted)
    decay_rate = (-jnp.exp(log_rate)).reshape(groups_here, per_group)
    x_spans = x_float.reshape(spans, SPAN, groups_here, per_group, HEAD_DIM)
    dt_spans = step_size.reshape(spans, SPAN, groups_here, per_group)
    b_spans = b_matrix.astype(jnp.float32).reshape(spans, SPAN, groups_here, STATE)
    c_spans = c_matrix.astype(jnp.float32).reshape(spans, SPAN, groups_here, STATE)
    segment = jnp.cumsum(doc_resets.reshape(spans, SPAN), axis=1, dtype=jnp.int32)

    def states_call(x_value, dt_value, b_value):
        return local_states(x_value, dt_value, b_value, segment, decay_rate)

    (starts, end_local, through_all), states_back = jax.vjp(states_call, x_spans, dt_spans, b_spans)
    identity = (jnp.ones_like(through_all), jnp.zeros_like(end_local))
    decay_table = lax.all_gather(through_all, "ctx", axis=0, tiled=True)
    own_index = lax.axis_index("ctx")
    ctx_count = lax.axis_size("ctx")
    flat_end = end_local.reshape(heads_here, HEAD_DIM, STATE)
    row_ids = jnp.arange(lax.axis_size("ctx") * heads_here, dtype=jnp.int32)
    receiver = row_ids // heads_here
    head_ids = row_ids % heads_here
    devices = jnp.arange(ctx_count, dtype=jnp.int32)
    between = (devices[None, :] > own_index) & (devices[None, :] < receiver[:, None])
    factors = jnp.where(between, decay_table[:, head_ids].T, 1.0)
    weight = jnp.prod(factors, axis=1) * (own_index < receiver).astype(jnp.float32)
    entry_state = lax.psum_scatter(
        weight[:, None, None] * jnp.take(flat_end, head_ids, axis=0),
        "ctx",
        scatter_dimension=0,
        tiled=True,
    ).reshape(end_local.shape)

    def output_call(x_value, dt_value, b_value, c_value, start_value, entry_value):
        return output_part(
            x_value, dt_value, b_value, c_value, segment, decay_rate, start_value, entry_value
        )

    core_part, output_back = jax.vjp(
        output_call, x_spans, dt_spans, b_spans, c_spans, starts, entry_state
    )
    skip_cols = jnp.repeat(skip_gain, HEAD_DIM)[None, :]
    core_out = core_part.reshape(tokens_here, heads_here * HEAD_DIM) + x_float * skip_cols
    gate_sig = jax.nn.sigmoid(gate_float)
    gate_act = gate_float * gate_sig
    gated = core_out * gate_act
    weighted_grad = norm_weight[None, :] * grad_output.astype(jnp.float32)
    norm_width = lax.axis_size("head") * gated.shape[1]
    squares = lax.psum(jnp.sum(gated * gated, axis=1), "head")
    inv_rms = lax.rsqrt(squares / norm_width + EPSILON)
    normed = gated * inv_rms[:, None]
    product = lax.psum(jnp.sum(weighted_grad * normed, axis=1), "head")
    grad_gated = inv_rms[:, None] * (weighted_grad - normed * (product / norm_width)[:, None])
    grad_core = grad_gated * gate_act
    grad_gate = grad_gated * core_out * gate_sig * (1.0 + gate_float * (1.0 - gate_sig))
    first_grads = output_back(grad_core.reshape(core_part.shape))
    _, exit_adjoint = carried_in((through_all, first_grads[5]), "ctx", compose, identity)
    through_grad = jnp.sum(exit_adjoint * entry_state, axis=(2, 3))
    second_grads = states_back((first_grads[4], exit_adjoint, through_grad))
    grad_input = (first_grads[0] + second_grads[0]).reshape(
        tokens_here, heads_here * HEAD_DIM
    ) + grad_core * skip_cols
    grad_step = (first_grads[1] + second_grads[1]).reshape(
        tokens_here, heads_here
    ) * jax.nn.sigmoid(shifted)
    grad_b_matrix = (first_grads[2] + second_grads[2]).reshape(tokens_here, groups_here * STATE)
    grad_c_matrix = first_grads[3].reshape(tokens_here, groups_here * STATE)
    return (
        grad_input.astype(jnp.bfloat16),
        grad_gate.astype(jnp.bfloat16),
        grad_step,
        grad_b_matrix,
        grad_c_matrix,
    )


def solution(mesh):
    return jax.shard_map(
        body,
        mesh=mesh,
        in_specs=(
            P("ctx", "head"),
            P("ctx", "head"),
            P("ctx", "head"),
            P("ctx", "head"),
            P("ctx", "head"),
            P("head"),
            P("head"),
            P("head"),
            P("head"),
            P("ctx"),
            P("ctx", "head"),
        ),
        out_specs=(
            P("ctx", "head"),
            P("ctx", "head"),
            P("ctx", "head"),
            P("ctx", "head"),
            P("ctx", "head"),
        ),
        check_vma=False,
    )
```

profile of v0, /device:TPU:1, one launch (start us, length us, event | category | flops | bytes accessed | tf_op | source)
XLA Modules:
  0.0 404.8 jit_solution(4905228115888977162)
XLA Ops:
  14.6 1.3 copy.242
  15.8 23.2 %all-gather = f32[32,1,1,16]{3,2,1,0:T(1,128)S(1)} all-gather(f32[1,1,1,16]{3,2,1,0:T(1,128)S(1)} %get-tuple-element.418), channel_id=2, replica_groups=mesh['ctx'=32,'head'=8] {'ctx'}, dimensions={0}, use_global_device_ids=true | all-gather | bytes 2112 | tf_op jit(solution)/shard_map/all_gather | solution.py:138
  39.1 1.5 fusion.46
  40.6 7.0 %gather_fusion.1 = f32[512,64,128]{2,1,0:T(8,128)} fusion(f32[16,64,128]{2,1,0:T(8,128)S(1)} %fusion.46, s32[1024]{0:T(1024)S(1)} %pad_clamp_fusion), kind=kCustom, calls=%fused_computation.1 | custom fusion | bytes 33556480 | tf_op jit(solution)/shard_map/jit(_take)/gather | solution.py:150
  47.6 1.0 gather_fusion
  48.9 11.9 %select_multiply_fusion = f32[512,64,128]{2,1,0:T(8,128)} fusion(f32[512,64,128]{2,1,0:T(8,128)} %gather_fusion.1, f32[512]{0:T(512)S(1)} %compare_select_fusion.3, pred[512]{0:T(512)(128)(4,1)S(1)} %compare_and_fusion), kind=kLoop, calls=%fused_computation.5 | loop fusion | flops 8388608 | bytes 33556992 | tf_op jit(solution)/shard_map/mul | solution.py:150
  62.6 120.6 %reduce-scatter.2.cloned.1.call-done = f32[16,64,128]{2,1,0:T(8,128)} async-done(((f32[512,64,128]{2,1,0:T(8,128)}), f32[16,64,128]{2,1,0:T(8,128)}) %reduce-scatter.2.cloned.1.call-update) | async-done | bytes 524304 | tf_op jit(solution)/shard_map/reduce_scatter | solution.py:149
  183.2 1.6 convolution_bitcast_fusion.1
  184.9 3.2 fusion.38
  189.1 14.0 %psum.14 = f32[256]{0:T(256)S(1)} all-reduce(f32[256]{0:T(256)S(1)} %get-tuple-element.406), channel_id=1, replica_groups=mesh['ctx'=32,'head'=8] {'head'}, use_global_device_ids=true, to_apply=%region_7.8 | all-reduce | flops 256 | bytes 2048 | tf_op jit(solution)/shard_map/psum | solution.py:171
  203.4 11.2 %psum.15 = f32[256]{0:T(256)S(1)} all-reduce(f32[256]{0:T(256)S(1)} %multiply_reduce_fusion.1), channel_id=1, replica_groups=mesh['ctx'=32,'head'=8] {'head'}, use_global_device_ids=true, to_apply=%region_9.10 | all-reduce | flops 256 | bytes 2048 | tf_op jit(solution)/shard_map/psum | solution.py:174
  214.6 3.0 fusion.56
  217.6 1.4 fusion.58
  219.0 1.1 convert.11
  221.0 2.0 multiply_reduce_fusion
  223.0 1.5 copy.259
  224.4 1.0 copy.279
  225.4 3.2 convolution_bitcast_fusion.3
  228.6 74.7 %all-gather.5.cloned.1.call-done = f32[512,64,128]{2,1,0:T(8,128)} async-done(((f32[16,64,128]{2,1,0:T(8,128)}), f32[512,64,128]{2,1,0:T(8,128)}) %all-gather.5.cloned.1.call-update) | async-done | bytes 16777232 | tf_op jit(solution)/shard_map/all_gather | solution.py:15
  303.4 59.4 %while.11 = (s32[]{:T(128)}, f32[1,16,64,128]{3,2,1,0:T(8,128)S(1)}, s32[]{:T(128)}, f32[32,1,16]{2,1,0:T(1,128)}, f32[32,1,16,64,128]{4,3,2,1,0:T(8,128)}, /*index=5*/s32[]{:T(128)}, s32[]{:T(128)}, s32[]{:T(128)}, s32[]{:T(128)}) while((s32[]{:T(128)}, f32[1,16,64,128]{3,2,1,0:T(8,128)S(1)}, s32[]{:T(128)}, ...), condition=%wide.region_11.12_spmd.clone, body=%wide.region_10.11_spmd.clone.sunk | while | flops 524296 | bytes 1573223 | solution.py:28
  304.1 1.2 fusion.115
  305.9 1.2 fusion.115
  307.8 1.2 fusion.115
  309.6 1.2 fusion.115
  311.5 1.2 fusion.115
  313.3 1.2 fusion.115
  315.2 1.2 fusion.115
  317.0 1.2 fusion.115
  318.9 1.2 fusion.115
  320.8 1.2 fusion.115
  322.6 1.2 fusion.115
  324.5 1.2 fusion.115
  326.3 1.2 fusion.115
  328.2 1.2 fusion.115
  330.0 1.2 fusion.115
  331.9 1.2 fusion.115
  333.7 1.2 fusion.115
  335.6 1.2 fusion.115
  337.4 1.2 fusion.115
  339.3 1.2 fusion.115
  341.2 1.2 fusion.115
  343.0 1.2 fusion.115
  344.9 1.2 fusion.115
  346.7 1.2 fusion.115
  348.6 1.2 fusion.115
  350.4 1.2 fusion.115
  352.3 1.2 fusion.115
  354.1 1.2 fusion.115
  356.0 1.2 fusion.115
  357.8 1.2 fusion.115
  359.7 1.2 fusion.115
  361.6 1.2 fusion.115
  362.8 1.6 fusion.50
  364.4 1.8 fusion.47
  366.9 8.3 %fusion.77 = (f32[16,256]{1,0:T(8,128)S(1)}, f32[16,256]{1,0:T(8,128)S(1)}, f32[16,256]{1,0:T(8,128)}, f32[256,256]{1,0:T(8,128)S(1)}) fusion(f32[16,256]{1,0:T(8,128)S(1)} %bitcast.277, f32[256,256]{1,0:T(8,128)S(1)} %fusion.81, f32[16,256]{1,0:T(8,128)S(1)} %bitcast.279, f32[256,256]{1,0:T(8,128)S(1)} %fusion.85, f32[256,1,16,64]{0,3,2,1:T(8,128)S(1)} %copy-done.8, ...), kind=kOutput, calls=%fused_computation.95 | convolution fusion | flops 825151488 | bytes 2965504 | tf_op jit(solution)/shard_map/transpose(jvp())/while/body/eval_jaxpr/checkpoint/ghts,sghp->tghp/dot_general | solution.py:41
  376.3 1.4 pad_add_fusion.1
  378.7 2.5 reduce-window.36
  381.3 2.7 reduce-window.34
  384.1 1.9 convolution_add_fusion
  386.1 1.2 fusion.49
  389.3 1.1 fusion.83
  390.5 1.4 bitcast_multiply_fusion.1
  391.9 4.8 %fusion.41 = f32[256,16,64]{0,2,1:T(8,128)S(1)} fusion(f32[16,256]{1,0:T(8,128)} %bitcast.280, f32[256,256]{1,0:T(8,128)} %copy-done.13, f32[16,256]{1,0:T(8,128)} %bitcast.276, f32[256,256]{1,0:T(8,128)} %copy-done.14, f32[256,1,16,64]{0,3,2,1:T(8,128)S(1)} %bitcast.251, f32[256,16,64]{0,2,1:T(8,128)S(1)} %copy-done.9, f32[256,16]{0,1:T(8,128)S(1)} %bitcast.264), kind=kOutput, calls=%fused_computation.47 | convolution fusion | flops 811073536 | bytes 3719168 | tf_op jit(solution)/shard_map/transpose(jvp())/while/body/eval_jaxpr/checkpoint/ghts,sghp->tghp/dot_general | solution.py:41
  397.0 1.0 copy.278
  (179 shorter events, 36.4 us)
Async XLA Ops:
  7.2 176.0 %reduce-scatter.2.cloned.1.call-start = ((), (), s32[]{:S(2)}) async-start(), calls=%async_computation.1 | async-start | bytes 17301504 | tf_op jit(solution)/shard_map/reduce_scatter | solution.py:149
  7.9 0.8 copy-start.32
  10.9 3.1 copy-start.30
  10.9 51.4 %copy-start.21 = (s32[256]{0:T(256)}, s32[256]{0:T(256)S(1)}, u32[]{:S(2)}) copy-start(s32[256]{0:T(256)S(1)} %get-tuple-element.298) | copy-start | bytes 3076
  14.0 33.6 %copy-start.29 = (f32[16]{0:T(128)}, f32[16]{0:T(128)S(1)}, u32[]{:S(2)}) copy-start(f32[16]{0:T(128)S(1)} %get-tuple-element.419) | copy-start | bytes 196
  14.1 1.7 copy-start.27
  39.0 8.5 %copy-start.20 = (f32[32,1,1,16]{3,2,1,0:T(1,128)}, f32[32,1,1,16]{3,2,1,0:T(1,128)S(1)}, u32[]{:S(2)}) copy-start(f32[32,1,1,16]{3,2,1,0:T(1,128)S(1)} %all-gather) | copy-start | bytes 6148
  60.8 0.7 copy-start.33
  60.8 1.1 copy-start.10
  60.8 1.3 copy-start.11
  60.8 1.6 copy-start.5
  60.8 1.6 copy-start.6
  60.8 242.6 %all-gather.5.cloned.1.call-start = ((), (), s32[]{:S(2)}) async-start(), calls=%async_computation.2 | async-start | bytes 17301504 | tf_op jit(solution)/shard_map/all_gather | solution.py:15
  60.9 127.2 %copy-start.24 = (f32[1,256,1,16]{1,3,2,0:T(8,128)}, f32[1,256,1,16]{1,3,2,0:T(8,128)S(1)}, u32[]{:S(2)}) copy-start(f32[1,256,1,16]{1,3,2,0:T(8,128)S(1)} %copy.248) | copy-start | bytes 49156
  61.4 156.1 %copy-start.15 = (f32[1,256,1,16]{1,3,2,0:T(8,128)}, f32[1,256,1,16]{1,3,2,0:T(8,128)S(1)}, u32[]{:S(2)}) copy-start(f32[1,256,1,16]{1,3,2,0:T(8,128)S(1)} %copy.254) | copy-start | bytes 49156
  61.8 152.8 %copy-start.18 = (f32[1024]{0:T(1024)}, f32[1024]{0:T(1024)S(1)}, u32[]{:S(2)}) copy-start(f32[1024]{0:T(1024)S(1)} %mul.544) | copy-start | bytes 12292
  62.0 126.1 %copy-start.1 = (bf16[256,1024]{0,1:T(8,128)(2,1)}, bf16[256,1024]{0,1:T(8,128)(2,1)S(1)}, u32[]{:S(2)}) copy-start(bf16[256,1024]{0,1:T(8,128)(2,1)S(1)} %copy.255) | copy-start | bytes 1572868
  184.8 3.7 copy-start.3
  184.8 18.3 %copy-start.23 = (f32[1024]{0:T(1024)S(1)}, f32[1024]{0:T(1024)}, u32[]{:S(2)}) copy-start(f32[1024]{0:T(1024)} %param.21) | copy-start | bytes 12292
  188.1 1.0 copy-start.2
  217.5 6.9 %copy-start.4 = (bf16[256,1024]{0,1:T(8,128)(2,1)S(1)}, bf16[256,1024]{0,1:T(8,128)(2,1)}, u32[]{:S(2)}) copy-start(bf16[256,1024]{0,1:T(8,128)(2,1)} %get-tuple-element.412) | copy-start | bytes 1572868
  217.6 7.9 %copy-start = (f32[16,64,128]{2,1,0:T(8,128)S(1)}, f32[16,64,128]{2,1,0:T(8,128)}, u32[]{:S(2)}) copy-start(f32[16,64,128]{2,1,0:T(8,128)} %reduce-scatter.2.cloned.1.call-done) | copy-start | bytes 1572868
  228.6 134.1 %copy-start.7 = (bf16[256,128]{1,0:T(8,128)(2,1)S(1)}, bf16[256,128]{1,0:T(8,128)(2,1)}, u32[]{:S(2)}) copy-start(bf16[256,128]{1,0:T(8,128)(2,1)} %param.16) | copy-start | bytes 196612
  303.4 62.8 %copy-start.17 = (f32[256,16]{0,1:T(8,128)S(1)}, f32[256,16]{0,1:T(8,128)}, u32[]{:S(2)}) copy-start(f32[256,16]{0,1:T(8,128)} %param.15) | copy-start | bytes 49156
  303.4 62.8 %copy-start.28 = (f32[256]{0:T(256)S(1)}, f32[256]{0:T(256)}, u32[]{:S(2)}) copy-start(f32[256]{0:T(256)} %copy-done.27) | copy-start | bytes 3076
  303.4 62.8 %copy-start.31 = (f32[16]{0:T(128)S(1)}, f32[16]{0:T(128)}, u32[]{:S(2)}) copy-start(f32[16]{0:T(128)} %param.18) | copy-start | bytes 196
  303.4 62.9 %copy-start.22 = (s32[256]{0:T(256)S(1)}, s32[256]{0:T(256)}, u32[]{:S(2)}) copy-start(s32[256]{0:T(256)} %copy-done.21) | copy-start | bytes 3076
  362.7 4.1 %copy-start.8 = (f32[256,1,16,64]{0,3,2,1:T(8,128)S(1)}, f32[256,1,16,64]{0,3,2,1:T(8,128)}, u32[]{:S(2)}) copy-start(f32[256,1,16,64]{0,3,2,1:T(8,128)} %convert.11) | copy-start | bytes 3145732
  362.7 4.1 %copy-start.25 = (f32[1,256,1,16]{1,3,2,0:T(8,128)S(1)}, f32[1,256,1,16]{1,3,2,0:T(8,128)}, u32[]{:S(2)}) copy-start(f32[1,256,1,16]{1,3,2,0:T(8,128)} %copy-done.24) | copy-start | bytes 49156
  364.3 2.5 copy-start.16
  366.3 8.9 %copy-start.26 = (f32[256,1,16]{0,2,1:T(8,128)}, f32[256,1,16]{0,2,1:T(8,128)S(1)}, u32[]{:S(2)}) copy-start(f32[256,1,16]{0,2,1:T(8,128)S(1)} %get-tuple-element.299) | copy-start | bytes 49156
  366.4 8.8 %copy-start.13 = (f32[256,256]{1,0:T(8,128)}, f32[256,256]{1,0:T(8,128)S(1)}, u32[]{:S(2)}) copy-start(f32[256,256]{1,0:T(8,128)S(1)} %fusion.81) | copy-start | bytes 786436
  366.8 8.4 %copy-start.14 = (f32[256,256]{1,0:T(8,128)}, f32[256,256]{1,0:T(8,128)S(1)}, u32[]{:S(2)}) copy-start(f32[256,256]{1,0:T(8,128)S(1)} %fusion.85) | copy-start | bytes 786436
  366.9 9.4 %copy-start.12 = (f32[1,256,1,16]{3,2,1,0:T(1,128)S(1)}, f32[1,256,1,16]{3,2,1,0:T(1,128)}, u32[]{:S(2)}) copy-start(f32[1,256,1,16]{3,2,1,0:T(1,128)} %copy.259) | copy-start | bytes 49156
  376.3 15.7 %copy-start.9 = (f32[256,16,64]{0,2,1:T(8,128)S(1)}, f32[256,16,64]{0,2,1:T(8,128)}, u32[]{:S(2)}) copy-start(f32[256,16,64]{0,2,1:T(8,128)} %get-tuple-element.426) | copy-start | bytes 3145732
  389.3 7.5 %copy-start.19 = (f32[1024]{0:T(1024)S(1)}, f32[1024]{0:T(1024)}, u32[]{:S(2)}) copy-start(f32[1024]{0:T(1024)} %copy-done.18) | copy-start | bytes 12292
Sparse Core Ops, SparseCore 0:
  60.9 122.2 reduce-scatter.1
  219.1 84.1 all-gather.4
where the time goes:
time: 408 us; the launch traced here: 405 us
  waiting for transfers between devices  195 us (48%)
  other arithmetic  72.1 us (18%)
  blocking collectives  48.4 us (12%)
  local copies, waits for them, and re-layouts  40.9 us (10%)
  matrix products  31.2 us (8%)
  between operations  15.9 us (4%)
    reduce_scatter x1, waiting for transfers between devices, body(): lax.psum_scatter(weight[:, None, None] * jnp.take(flat_end, head_ids, axi...  121 us
    all_gather x1, waiting for transfers between devices, carried_in(): everything = jax.tree.map(lambda part: lax.all_gather(part, axis), array)  74.7 us
    select_n x32, other arithmetic, turn(): return jax.tree.map(lambda a, b: jnp.where(reached, a, b), new, before)  37.4 us
    all_gather x1, blocking collectives, body(): decay_table = lax.all_gather(through_all, 'ctx', axis=0, tiled=True)  23.2 us
    mul x32, local copies, waits for them, and re-layouts, compose(): decay_late[..., None, None] * sum_early + sum_late  21.1 us
    dot_general x3, matrix products, span_mix(): jnp.einsum('ghts,sghp->tghp', weights, x_span, precision=HIGHEST_PRECISION)  16.4 us
    psum x1, blocking collectives, body(): squares = lax.psum(jnp.sum(gated * gated, axis=1), 'head')  14 us
    mul x1, other arithmetic, body(): weight[:, None, None] * jnp.take(flat_end, head_ids, axis=0)  11.9 us
  transfers between devices with their start and end apart: 2, of which 2 were waited for; matrix products, arithmetic and copies ran while one was open for 3% of the time, Pallas kernels for 0%

commit v1 on v0

--- a/solution.py
+++ b/solution.py
@@ -114,6 +114,12 @@
     doc_resets,
     grad_output,
 ):
+
+    def group_the_trails(content):
+        return jnp.concatenate(
+            lax.all_to_all(jnp.stack(lax.axis_size("ctx") * [content], 0), "ctx", 0, 0), 0
+        )
+
     tokens_here = ssm_input.shape[0]
     heads_here = step_raw.shape[1]
     groups_here = b_matrix.shape[1] // STATE
@@ -135,7 +141,7 @@
 
     (starts, end_local, through_all), states_back = jax.vjp(states_call, x_spans, dt_spans, b_spans)
     identity = (jnp.ones_like(through_all), jnp.zeros_like(end_local))
-    decay_table = lax.all_gather(through_all, "ctx", axis=0, tiled=True)
+    decay_table = group_the_trails(through_all)
     own_index = lax.axis_index("ctx")
     ctx_count = lax.axis_size("ctx")
     flat_end = end_local.reshape(heads_here, HEAD_DIM, STATE)

time: 408 us -> 380 us (0.931)
  waiting for transfers between devices: 195 us -> 157 us
  starting transfers between devices: 0.08 us -> 8.66 us
  blocking collectives: 48.4 us -> 56.8 us
    all_gather x1, waiting for transfers between devices: 74.7 us -> 34.9 us  [carried_in(): everything = jax.tree.map(lambda part: lax.all_gather(part, axis), array)]
    all_to_all x0 -> x1, starting transfers between devices: none -> 8.58 us  [group_the_trails(): lax.all_to_all(jnp.stack(lax.axis_size('ctx') * [content], 0), 'ctx', 0, 0)]
    all_gather x1, blocking collectives: 23.2 us -> 31.5 us  [carried_in(): everything = jax.tree.map(lambda part: lax.all_gather(part, axis), array)]
  transfers between devices with their start and end apart: 2 -> 3, of which waited for: 2 -> 2; matrix products, arithmetic and copies ran while one was open for 3% -> 8% of each run, Pallas kernels for 0% -> 0%
where the time goes in v1:
time: 380 us; the launch traced here: 377 us
  waiting for transfers between devices  157 us (41%)
  other arithmetic  69.8 us (18%)
  blocking collectives  56.8 us (15%)
  local copies, waits for them, and re-layouts  37 us (10%)
  matrix products  30.8 us (8%)
  between operations  15.9 us (4%)
  starting transfers between devices  8.66 us (2%)
    reduce_scatter x1, waiting for transfers between devices, body(): lax.psum_scatter(weight[:, None, None] * jnp.take(flat_end, head_ids, axi...  123 us
    select_n x32, other arithmetic, turn(): return jax.tree.map(lambda a, b: jnp.where(reached, a, b), new, before)  37.4 us
    all_gather x1, waiting for transfers between devices, carried_in(): everything = jax.tree.map(lambda part: lax.all_gather(part, axis), array)  34.9 us
    all_gather x1, blocking collectives, carried_in(): everything = jax.tree.map(lambda part: lax.all_gather(part, axis), array)  31.5 us
    mul x32, local copies, waits for them, and re-layouts, compose(): decay_late[..., None, None] * sum_early + sum_late  20.4 us
    dot_general x3, matrix products, span_mix(): jnp.einsum('ghts,sghp->tghp', weights, x_span, precision=HIGHEST_PRECISION)  17.4 us
    psum x1, blocking collectives, body(): squares = lax.psum(jnp.sum(gated * gated, axis=1), 'head')  13.9 us
    mul x1, other arithmetic, body(): weight[:, None, None] * jnp.take(flat_end, head_ids, axis=0)  11.9 us
  transfers between devices with their start and end apart: 3, of which 2 were waited for; matrix products, arithmetic and copies ran while one was open for 8% of the time, Pallas kernels for 0%

profile of v1, /device:TPU:1, one launch (start us, length us, event | category | flops | bytes accessed | tf_op | source)
XLA Modules:
  0.0 377.4 jit_solution(2483100314060556413)
XLA Ops:
  7.8 1.4 fusion.113
  10.0 1.0 reduce-window.30
  15.7 8.6 %all-to-all-start = ((f32[32,1,16]{2,1,0:T(1,128)}), f32[32,1,16]{2,1,0:T(1,128)S(1)}, u32[]{:S(2)}, u32[]{:S(2)}) async-start(f32[32,1,16]{2,1,0:T(1,128)} %stack.2), calls=%async_computation | async-start | bytes 32768 | tf_op jit(solution)/shard_map/all_to_all | solution.py:120
  25.2 1.2 copy.113
  26.5 1.5 fusion.46
  28.0 7.0 %gather_fusion.1 = f32[512,64,128]{2,1,0:T(8,128)} fusion(f32[16,64,128]{2,1,0:T(8,128)S(1)} %fusion.46, s32[1024]{0:T(1024)S(1)} %pad_clamp_fusion), kind=kCustom, calls=%fused_computation.1 | custom fusion | bytes 33556480 | tf_op jit(solution)/shard_map/jit(_take)/gather | solution.py:156
  35.0 1.0 gather_fusion
  36.3 11.9 %select_multiply_fusion = f32[512,64,128]{2,1,0:T(8,128)} fusion(f32[512,64,128]{2,1,0:T(8,128)} %gather_fusion.1, f32[512]{0:T(512)S(1)} %compare_select_fusion.3, pred[512]{0:T(512)(128)(4,1)S(1)} %compare_and_fusion), kind=kLoop, calls=%fused_computation.5 | loop fusion | flops 8388608 | bytes 33556992 | tf_op jit(solution)/shard_map/mul | solution.py:156
  50.0 122.6 %reduce-scatter.2.cloned.1.call-done = f32[16,64,128]{2,1,0:T(8,128)} async-done(((f32[512,64,128]{2,1,0:T(8,128)}), f32[16,64,128]{2,1,0:T(8,128)}) %reduce-scatter.2.cloned.1.call-update) | async-done | bytes 524304 | tf_op jit(solution)/shard_map/reduce_scatter | solution.py:155
  172.7 1.6 convolution_bitcast_fusion.1
  174.3 3.2 fusion.38
  178.5 13.9 %psum.14 = f32[256]{0:T(256)S(1)} all-reduce(f32[256]{0:T(256)S(1)} %get-tuple-element.388), channel_id=1, replica_groups=mesh['ctx'=32,'head'=8] {'head'}, use_global_device_ids=true, to_apply=%region_7.8 | all-reduce | flops 256 | bytes 2048 | tf_op jit(solution)/shard_map/psum | solution.py:177
  192.7 11.3 %psum.15 = f32[256]{0:T(256)S(1)} all-reduce(f32[256]{0:T(256)S(1)} %multiply_reduce_fusion.1), channel_id=1, replica_groups=mesh['ctx'=32,'head'=8] {'head'}, use_global_device_ids=true, to_apply=%region_9.10 | all-reduce | flops 256 | bytes 2048 | tf_op jit(solution)/shard_map/psum | solution.py:180
  204.1 3.2 fusion.56
  207.3 1.4 fusion.58
  208.8 1.1 convert.11
  209.9 31.5 %all-gather = f32[32,1,1,16]{3,2,1,0:T(1,128)} all-gather(f32[1,1,1,16]{3,2,1,0:T(1,128)S(1)} %copy.123), channel_id=2, replica_groups=mesh['ctx'=32,'head'=8] {'ctx'}, dimensions={0}, use_global_device_ids=true | all-gather | bytes 2112 | tf_op jit(solution)/shard_map/all_gather | solution.py:15
  241.5 1.0 copy.139
  242.5 2.6 convolution_bitcast_fusion.3
  245.1 1.4 multiply_reduce_fusion
  247.8 9.1 %fusion.77 = (f32[16,256]{1,0:T(8,128)}, f32[16,256]{1,0:T(8,128)}, f32[16,256]{1,0:T(8,128)}, f32[256,256]{1,0:T(8,128)S(1)}) fusion(f32[16,256]{1,0:T(8,128)S(1)} %bitcast.286, f32[256,256]{1,0:T(8,128)S(1)} %fusion.81, f32[16,256]{1,0:T(8,128)} %bitcast.296, f32[256,256]{1,0:T(8,128)S(1)} %fusion.84, f32[256,1,16,64]{0,3,2,1:T(8,128)S(1)} %copy-done.8, ...), kind=kOutput, calls=%fused_computation.95 | convolution fusion | flops 825151488 | bytes 2965504 | tf_op jit(solution)/shard_map/transpose(jvp())/while/body/eval_jaxpr/checkpoint/ghts,sghp->tghp/dot_general | solution.py:41
  256.8 1.0 convolution_add_fusion
  257.9 34.9 %all-gather.4.cloned.1.call-done = f32[512,64,128]{2,1,0:T(8,128)} async-done(((f32[16,64,128]{2,1,0:T(8,128)}), f32[512,64,128]{2,1,0:T(8,128)}) %all-gather.4.cloned.1.call-update) | async-done | bytes 16777232 | tf_op jit(solution)/shard_map/all_gather | solution.py:15
  292.7 58.8 %while.11 = (s32[]{:T(128)}, f32[1,16,64,128]{3,2,1,0:T(8,128)S(1)}, s32[]{:T(128)}, f32[32,1,16]{2,1,0:T(1,128)}, f32[32,1,16,64,128]{4,3,2,1,0:T(8,128)}, /*index=5*/s32[]{:T(128)}, s32[]{:T(128)}, s32[]{:T(128)}, s32[]{:T(128)}) while((s32[]{:T(128)}, f32[1,16,64,128]{3,2,1,0:T(8,128)S(1)}, s32[]{:T(128)}, ...), condition=%wide.region_11.12_spmd.clone, body=%wide.region_10.11_spmd.clone.sunk | while | flops 524296 | bytes 1573231 | solution.py:28
  293.3 1.2 fusion.126
  295.2 1.2 fusion.126
  297.1 1.2 fusion.126
  298.9 1.2 fusion.126
  300.7 1.2 fusion.126
  302.5 1.2 fusion.126
  304.3 1.2 fusion.126
  306.1 1.2 fusion.126
  308.0 1.2 fusion.126
  309.9 1.2 fusion.126
  311.7 1.2 fusion.126
  313.6 1.2 fusion.126
  315.4 1.2 fusion.126
  317.3 1.2 fusion.126
  319.1 1.2 fusion.126
  320.9 1.2 fusion.126
  322.7 1.2 fusion.126
  324.6 1.2 fusion.126
  326.4 1.2 fusion.126
  328.2 1.2 fusion.126
  330.1 1.2 fusion.126
  331.9 1.2 fusion.126
  333.7 1.2 fusion.126
  335.6 1.2 fusion.126
  337.4 1.2 fusion.126
  339.3 1.2 fusion.126
  341.1 1.2 fusion.126
  342.9 1.2 fusion.126
  344.8 1.2 fusion.126
  346.7 1.2 fusion.126
  348.5 1.2 fusion.126
  350.4 1.2 fusion.126
  351.6 1.8 fusion.47
  353.4 1.6 fusion.50
  355.4 1.0 fusion.115
  356.5 2.5 reduce-window.36
  359.1 2.5 reduce-window.34
  361.7 1.3 fusion.49
  363.0 5.1 %fusion.41 = f32[256,16,64]{0,2,1:T(8,128)S(1)} fusion(f32[16,256]{1,0:T(8,128)} %bitcast.297, f32[256,256]{1,0:T(8,128)S(1)} %copy-done.13, f32[16,256]{1,0:T(8,128)S(1)} %bitcast.288, f32[256,256]{1,0:T(8,128)} %copy-done.14, f32[256,1,16,64]{0,3,2,1:T(8,128)S(1)} %bitcast.279, f32[256,16,64]{0,2,1:T(8,128)} %get-tuple-element.406, ...), kind=kOutput, calls=%fused_computation.47 | convolution fusion | flops 811073536 | bytes 3719168 | tf_op jit(solution)/shard_map/transpose(jvp())/while/body/eval_jaxpr/checkpoint/ghts,sghp->tghp/dot_general | solution.py:41
  368.3 1.0 copy.138
  (171 shorter events, 32.9 us)
Async XLA Ops:
  7.8 1.4 copy-start.29
  12.0 2.2 copy-start.27
  12.0 37.7 %copy-start.20 = (s32[256]{0:T(256)}, s32[256]{0:T(256)S(1)}, u32[]{:S(2)}) copy-start(s32[256]{0:T(256)S(1)} %get-tuple-element.298) | copy-start | bytes 3076
  14.2 193.0 %copy-start.17 = (f32[256,16]{0,1:T(8,128)}, f32[256,16]{0,1:T(8,128)S(1)}, u32[]{:S(2)}) copy-start(f32[256,16]{0,1:T(8,128)S(1)} %get-tuple-element.390) | copy-start | bytes 49156
  15.0 19.9 %copy-start.25 = (f32[16]{0:T(128)}, f32[16]{0:T(128)S(1)}, u32[]{:S(2)}) copy-start(f32[16]{0:T(128)S(1)} %get-tuple-element.404) | copy-start | bytes 196
  15.7 19.3 %all-to-all-start = ((f32[32,1,16]{2,1,0:T(1,128)}), f32[32,1,16]{2,1,0:T(1,128)S(1)}, u32[]{:S(2)}, u32[]{:S(2)}) async-start(f32[32,1,16]{2,1,0:T(1,128)} %stack.2), calls=%async_computation | async-start | bytes 32768 | tf_op jit(solution)/shard_map/all_to_all | solution.py:120
  24.3 148.4 %reduce-scatter.2.cloned.1.call-start = ((), (), s32[]{:S(2)}) async-start(), calls=%async_computation.2 | async-start | bytes 17301504 | tf_op jit(solution)/shard_map/reduce_scatter | solution.py:155
  24.4 10.6 %copy-start.22 = (f32[256]{0:T(256)}, f32[256]{0:T(256)S(1)}, u32[]{:S(2)}) copy-start(f32[256]{0:T(256)S(1)} %compare_convert_fusion.1) | copy-start | bytes 3076
  25.2 9.8 %copy-start.15 = (f32[256,16]{0,1:T(8,128)}, f32[256,16]{0,1:T(8,128)S(1)}, u32[]{:S(2)}) copy-start(f32[256,16]{0,1:T(8,128)S(1)} %fusion.98) | copy-start | bytes 49156
  48.2 0.7 copy-start.31
  48.2 1.1 copy-start.9
  48.2 1.3 copy-start.10
  48.2 1.6 copy-start.6
  48.2 1.6 copy-start.7
  48.3 244.5 %all-gather.4.cloned.1.call-start = ((), (), s32[]{:S(2)}) async-start(), calls=%async_computation.3 | async-start | bytes 17301504 | tf_op jit(solution)/shard_map/all_gather | solution.py:15
  49.3 154.8 %copy-start.18 = (f32[1024]{0:T(1024)}, f32[1024]{0:T(1024)S(1)}, u32[]{:S(2)}) copy-start(f32[1024]{0:T(1024)S(1)} %mul.534) | copy-start | bytes 12292
  49.5 128.0 %copy-start.2 = (bf16[256,1024]{0,1:T(8,128)(2,1)}, bf16[256,1024]{0,1:T(8,128)(2,1)S(1)}, u32[]{:S(2)}) copy-start(bf16[256,1024]{0,1:T(8,128)(2,1)S(1)} %copy.120) | copy-start | bytes 1572868
  49.7 142.7 %copy-start.1 = (bf16[256,1024]{0,1:T(8,128)(2,1)}, bf16[256,1024]{0,1:T(8,128)(2,1)S(1)}, u32[]{:S(2)}) copy-start(bf16[256,1024]{0,1:T(8,128)(2,1)S(1)} %copy.121) | copy-start | bytes 1572868
  174.3 3.7 copy-start.4
  174.3 18.2 %copy-start.21 = (f32[1024]{0:T(1024)S(1)}, f32[1024]{0:T(1024)}, u32[]{:S(2)}) copy-start(f32[1024]{0:T(1024)} %param.21) | copy-start | bytes 12292
  177.5 1.0 copy-start.3
  204.1 38.4 %copy-start = (f32[16,64,128]{2,1,0:T(8,128)S(1)}, f32[16,64,128]{2,1,0:T(8,128)}, u32[]{:S(2)}) copy-start(f32[16,64,128]{2,1,0:T(8,128)} %reduce-scatter.2.cloned.1.call-done) | copy-start | bytes 1572868
  207.3 34.2 %copy-start.5 = (bf16[256,1024]{0,1:T(8,128)(2,1)S(1)}, bf16[256,1024]{0,1:T(8,128)(2,1)}, u32[]{:S(2)}) copy-start(bf16[256,1024]{0,1:T(8,128)(2,1)} %get-tuple-element.396) | copy-start | bytes 1572868
  242.5 5.3 %copy-start.8 = (f32[256,1,16,64]{0,3,2,1:T(8,128)S(1)}, f32[256,1,16,64]{0,3,2,1:T(8,128)}, u32[]{:S(2)}) copy-start(f32[256,1,16,64]{0,3,2,1:T(8,128)} %convert.11) | copy-start | bytes 3145732
  247.3 9.5 %copy-start.12 = (f32[256,256]{1,0:T(8,128)}, f32[256,256]{1,0:T(8,128)S(1)}, u32[]{:S(2)}) copy-start(f32[256,256]{1,0:T(8,128)S(1)} %fusion.81) | copy-start | bytes 786436
  247.7 9.1 %copy-start.14 = (f32[256,256]{1,0:T(8,128)}, f32[256,256]{1,0:T(8,128)S(1)}, u32[]{:S(2)}) copy-start(f32[256,256]{1,0:T(8,128)S(1)} %fusion.84) | copy-start | bytes 786436
  257.9 93.7 %copy-start.16 = (f32[256,16]{0,1:T(8,128)S(1)}, f32[256,16]{0,1:T(8,128)}, u32[]{:S(2)}) copy-start(f32[256,16]{0,1:T(8,128)} %copy-done.15) | copy-start | bytes 49156
  351.5 3.8 %copy-start.11 = (f32[256,16]{0,1:T(8,128)S(1)}, f32[256,16]{0,1:T(8,128)}, u32[]{:S(2)}) copy-start(f32[256,16]{0,1:T(8,128)} %param.15) | copy-start | bytes 49156
  351.6 11.4 %copy-start.13 = (f32[256,256]{1,0:T(8,128)S(1)}, f32[256,256]{1,0:T(8,128)}, u32[]{:S(2)}) copy-start(f32[256,256]{1,0:T(8,128)} %copy-done.12) | copy-start | bytes 786436
  355.2 12.9 %copy-start.19 = (f32[1024]{0:T(1024)S(1)}, f32[1024]{0:T(1024)}, u32[]{:S(2)}) copy-start(f32[1024]{0:T(1024)} %copy-done.18) | copy-start | bytes 12292
  363.0 6.8 %copy-start.23 = (f32[256]{0:T(256)S(1)}, f32[256]{0:T(256)}, u32[]{:S(2)}) copy-start(f32[256]{0:T(256)} %copy-done.22) | copy-start | bytes 3076
  363.0 6.8 %copy-start.24 = (f32[16,256]{1,0:T(8,128)S(1)}, f32[16,256]{1,0:T(8,128)}, u32[]{:S(2)}) copy-start(f32[16,256]{1,0:T(8,128)} %get-tuple-element.372) | copy-start | bytes 49156
  363.0 6.8 %copy-start.26 = (f32[16]{0:T(128)S(1)}, f32[16]{0:T(128)}, u32[]{:S(2)}) copy-start(f32[16]{0:T(128)} %copy-done.25) | copy-start | bytes 196
  363.0 6.9 %copy-start.28 = (f32[16]{0:T(128)S(1)}, f32[16]{0:T(128)}, u32[]{:S(2)}) copy-start(f32[16]{0:T(128)} %param.18) | copy-start | bytes 196
  363.0 6.8 %copy-start.30 = (f32[16]{0:T(128)S(1)}, f32[16]{0:T(128)}, u32[]{:S(2)}) copy-start(f32[16]{0:T(128)} %copy-done.29) | copy-start | bytes 196
Sparse Core Ops, SparseCore 0:
  48.4 124.2 reduce-scatter.1
  208.8 83.8 all-gather.3
